TPU v7x, 512 devices: a whole 4x8x8 slice. The times are simulated.
512 devices in a mesh: resp: 64 (over y_lo, z, core), mp: 8 (over y_hi, x).
Axes of the slice: x: 4, y: 8 (y_hi: 2, y_lo: 4; y = y_hi * 4 + y_lo), z: 8, core: 2. Of those that a mesh axis runs over, the one named last changes fastest.
Arguments:
- queries: bfloat16 [16384, 64, 128], P('resp', 'mp'), may hold values from -200 to 200
- response_kv: bfloat16 [16384, 2, 8, 128], P('resp', None, 'mp'), may hold values from -6 to 6
- prefix_kv: bfloat16 [4096, 2, 8, 128], P(('resp', 'mp')), may hold values from -8 to 8
- lengths: int32 [64], P('resp'), may hold values from 128 to 256, as said below
- score_weight: float32 [8192], P('mp'), may hold values from -30 to 30
Outputs:
- attended: bfloat16 [16384, 8192], P('resp', 'mp')
- score: float32 [64], P('resp')
Inputs may be any that keep to these rules, and one draw needn't show every extreme that they name: `lengths`: every length is a multiple of 128; some response is full and some has one tile.
All inputs are finite; a program needn't handle non-finite values.
Results may differ from a plain program's by a relative error of at most 0.0045.
Values may be sent and summed in bfloat16 or wider, within the bound.
No kernel may reach another device: no remote copies, remote signals or barrier semaphores. Data moves between devices by JAX's collectives and lax.ppermute only.
A program may use at most 64 MiB of HBM per device.

v0:
```python
import math
import jax
import jax.numpy as jnp
from jax import lax
from jax.sharding import PartitionSpec as P

neg_large = -1e30


def absorb(carry, keys, values, grouped, factor):
    best, total, accum = carry
    scores = jnp.einsum("grd,sgd->grs", grouped, keys, preferred_element_type=jnp.float32) * factor
    fresh = jnp.maximum(best, jnp.max(scores, axis=-1, keepdims=True))
    shrink = jnp.exp(best - fresh)
    weights = jnp.exp(scores - fresh)
    total = total * shrink + jnp.sum(weights, axis=-1, keepdims=True)
    accum = accum * shrink + jnp.einsum(
        "grs,sgd->grd", weights.astype(jnp.bfloat16), values, preferred_element_type=jnp.float32
    )
    return (fresh, total, accum)


def sweep(carry, whole_cache, grouped, factor):
    count = whole_cache.shape[0]
    block_len = math.gcd(count, 512)
    blocks = whole_cache.reshape((count // block_len, block_len) + whole_cache.shape[1:])

    def one_block(state, block):
        return (absorb(state, block[:, 0], block[:, 1], grouped, factor), None)

    carry, unused = lax.scan(one_block, carry, blocks)
    return carry


def per_device(queries, response_kv, prefix_kv, lengths, score_weight):
    resp_len = queries.shape[0]
    local_heads = queries.shape[1]
    head_size = queries.shape[2]
    local_kv = response_kv.shape[2]
    group = local_heads // local_kv
    rows = group * resp_len
    factor = 1.0 / math.sqrt(head_size)
    length = lengths[0]
    grouped = jnp.transpose(
        queries.reshape(resp_len, local_kv, group, head_size), (1, 2, 0, 3)
    ).reshape(local_kv, rows, head_size)
    key_pos = jnp.arange(resp_len, dtype=jnp.int32)[None, :]
    query_pos = (jnp.arange(rows, dtype=jnp.int32) % resp_len)[:, None]
    allowed = ((key_pos <= query_pos) & (key_pos < length))[None]
    near = (
        jnp.einsum("grd,sgd->grs", grouped, response_kv[:, 0], preferred_element_type=jnp.float32)
        * factor
    )
    near = jnp.where(allowed, near, neg_large)
    best = jnp.max(near, axis=-1, keepdims=True)
    near_w = jnp.where(allowed, jnp.exp(near - best), 0.0)
    total = jnp.sum(near_w, axis=-1, keepdims=True)
    accum = jnp.einsum(
        "grs,sgd->grd",
        near_w.astype(jnp.bfloat16),
        response_kv[:, 1],
        preferred_element_type=jnp.float32,
    )
    start_state = (best, total, accum)
    mine = lax.all_to_all(prefix_kv, "mp", split_axis=2, concat_axis=0, tiled=True)
    collected = lax.all_gather(mine, "resp", axis=0, tiled=True)
    best, total, accum = sweep(start_state, collected, grouped, factor)
    mixed = (accum / total).reshape(local_kv, group, resp_len, head_size)
    mixed = jnp.transpose(mixed, (2, 0, 1, 3)).reshape(resp_len, local_heads * head_size)
    live = jnp.arange(resp_len, dtype=jnp.int32)[:, None] < length
    attended = jnp.where(live, mixed, 0.0).astype(jnp.bfloat16)
    partial_score = jnp.sum(attended.astype(jnp.float32) * score_weight[None, :])
    summed = lax.psum(partial_score, "mp")
    score = (summed / length.astype(jnp.float32)).reshape(1)
    return (attended, score)


def solution(mesh):
    in_specs = (
        P("resp", "mp", None),
        P("resp", None, "mp", None),
        P(("resp", "mp"), None, None, None),
        P("resp"),
        P("mp"),
    )
    out_specs = (P("resp", "mp"), P("resp"))
    return jax.shard_map(
        per_device, mesh=mesh, in_specs=in_specs, out_specs=out_specs, check_vma=False
    )
```

profile of v0, /device:TPU:8, one launch (start us, length us, event | category | flops | bytes accessed | tf_op | source)
XLA Modules:
  0.0 215.8 jit_solution(12020379419026221911)
XLA Ops:
  8.0 18.6 %all_to_all.18 = bf16[8,2,8,128]{3,0,1,2:T(8,128)(2,1)S(1)} all-to-all(bf16[8,2,8,128]{3,0,1,2:T(8,128)(2,1)S(1)} %copy.18), channel_id=1, replica_groups=mesh['resp'=64,'mp'=8] {'mp'}, dimensions={2} | all-to-all | bytes 65536 | tf_op jit(solution)/shard_map/all_to_all | solution.py:65
  27.9 1.1 copy.15
  29.0 1.2 fusion.24
  31.7 1.0 convolution_bitcast_fusion.1
  32.6 110.5 %all-gather.2.cloned.1.call-done = bf16[4096,2,1,128]{3,0,1,2:T(8,128)(2,1)} async-done(((bf16[64,2,1,128]{3,0,1,2:T(8,128)(2,1)}), bf16[4096,2,1,128]{3,0,1,2:T(8,128)(2,1)}) %all-gather.2.cloned.1.call-update) | async-done | bytes 2097168 | tf_op jit(solution)/shard_map/all_gather | solution.py:66
  143.2 29.5 %while.14 = (s32[]{:T(128)}, f32[1,2048,1]{1,2,0:T(1,128)S(1)}, f32[1,2048,1]{1,2,0:T(1,128)S(1)}, f32[1,2048,128]{2,1,0:T(8,128)S(1)}, bf16[8,512,2,1,128]{4,1,...) while((s32[]{:T(128)}, f32[1,2048,1]{1,2,0:T(1,128)S(1)}, f32[1,2048,1]{1,2,0:T(1,128)S(1)}, ...), condition=%wide.region_5.6_spmd, body=%wide.region_2.5_spmd.sunk | while | flops 545787904 | bytes 16121945 | solution.py:31
  143.2 1.0 dynamic-slice_bitcast_fusion.2
  145.7 1.2 fusion.32
  146.9 1.0 dynamic-slice_bitcast_fusion.2
  149.3 1.2 fusion.32
  150.6 1.0 dynamic-slice_bitcast_fusion.2
  153.0 1.2 fusion.32
  154.2 1.0 dynamic-slice_bitcast_fusion.2
  156.7 1.2 fusion.32
  157.9 1.0 dynamic-slice_bitcast_fusion.2
  160.4 1.2 fusion.32
  161.6 1.0 dynamic-slice_bitcast_fusion.2
  164.1 1.2 fusion.32
  165.3 1.0 dynamic-slice_bitcast_fusion.2
  167.8 1.2 fusion.32
  169.0 1.0 dynamic-slice_bitcast_fusion.2
  171.5 1.2 fusion.32
  173.0 1.0 multiply_reduce_fusion.1
  174.4 31.9 %psum.7 = f32[]{:T(128)} all-reduce(f32[]{:T(128)} %multiply_reduce_fusion.1), channel_id=1, replica_groups=mesh['resp'=64,'mp'=8] {'mp'}, use_global_device_ids=true, to_apply=%region_7.8 | all-reduce | flops 1 | bytes 8 | tf_op jit(solution)/shard_map/psum | solution.py:73
  (53 shorter events, 16.3 us)
Async XLA Ops:
  7.2 136.0 %all-gather.2.cloned.1.call-start = ((), (), s32[]{:S(2)}) async-start(), calls=%async_computation.1 | async-start | bytes 2129920 | tf_op jit(solution)/shard_map/all_gather | solution.py:66
  143.2 29.8 %copy-start = (f32[1024]{0:T(1024)S(1)}, f32[1024]{0:T(1024)}, u32[]{:S(2)}) copy-start(f32[1024]{0:T(1024)} %param.11) | copy-start | bytes 12292
Sparse Core Ops, SparseCore 0:
  27.4 115.7 all-gather.1
where the time goes:
time: 216 us
  waiting for transfers between devices  111 us (51%)
  blocking collectives  50.5 us (23%)
  matrix products  16.9 us (8%)
  between operations  16.5 us (8%)
  local copies, waits for them, and re-layouts  11.9 us (6%)
  other arithmetic  9.04 us (4%)
    all_gather x1, waiting for transfers between devices, per_device(): collected = lax.all_gather(mine, 'resp', axis=0, tiled=True)  111 us
    psum x1, blocking collectives, per_device(): summed = lax.psum(partial_score, 'mp')  31.9 us
    all_to_all x1, blocking collectives, per_device(): lax.all_to_all(prefix_kv, 'mp', split_axis=2, concat_axis=0, tiled=True)  18.6 us
    dot_general x8, matrix products, absorb(): jnp.einsum('grs,sgd->grd', weights.astype(jnp.bfloat16), values, preferre...  9.46 us
    squeeze x8, local copies, waits for them, and re-layouts, sweep(): carry, unused = lax.scan(one_block, carry, blocks)  7.82 us
    dot_general x8, matrix products, absorb(): jnp.einsum('grd,sgd->grs', grouped, keys, preferred_element_type=jnp.floa...  5.75 us
    reduce_sum x8, other arithmetic, absorb(): total = total * shrink + jnp.sum(weights, axis=-1, keepdims=True)  5.68 us
  transfers between devices with their start and end apart: 1, of which 1 were waited for; matrix products, arithmetic and copies ran while one was open for 2% of the time, Pallas kernels for 0%

commit v1 on v0

--- a/solution.py
+++ b/solution.py
@@ -63,7 +63,9 @@
     )
     start_state = (best, total, accum)
     mine = lax.all_to_all(prefix_kv, "mp", split_axis=2, concat_axis=0, tiled=True)
-    collected = lax.all_gather(mine, "resp", axis=0, tiled=True)
+    collected = jnp.concatenate(
+        lax.all_to_all(jnp.stack([mine] * lax.axis_size("resp")), "resp", 0, 0), axis=0
+    )
     best, total, accum = sweep(start_state, collected, grouped, factor)
     mixed = (accum / total).reshape(local_kv, group, resp_len, head_size)
     mixed = jnp.transpose(mixed, (2, 0, 1, 3)).reshape(resp_len, local_heads * head_size)

time: 216 us -> 155 us (0.72)
  the two profiles are of different devices: /device:TPU:8 before, /device:TPU:56 now
where the time goes in v1:
time: 155 us; the launch traced here: 154 us
  waiting for transfers between devices  49.9 us (32%)
  blocking collectives  45.8 us (30%)
  matrix products  16.9 us (11%)
  starting transfers between devices  14.7 us (9%)
  local copies, waits for them, and re-layouts  14.1 us (9%)
  other arithmetic  9.04 us (6%)
  between operations  3.17 us (2%)
    all_to_all x1, waiting for transfers between devices, per_device(): lax.all_to_all(jnp.stack([mine] * lax.axis_size('resp')), 'resp', 0, 0)  49.9 us
    psum x1, blocking collectives, per_device(): summed = lax.psum(partial_score, 'mp')  31.5 us
    all_to_all x1, starting transfers between devices, per_device(): lax.all_to_all(jnp.stack([mine] * lax.axis_size('resp')), 'resp', 0, 0)  14.7 us
    all_to_all x1, blocking collectives, per_device(): lax.all_to_all(prefix_kv, 'mp', split_axis=2, concat_axis=0, tiled=True)  14.3 us
    dot_general x8, matrix products, absorb(): jnp.einsum('grs,sgd->grd', weights.astype(jnp.bfloat16), values, preferre...  9.46 us
    squeeze x8, local copies, waits for them, and re-layouts, sweep(): carry, unused = lax.scan(one_block, carry, blocks)  7.82 us
    dot_general x8, matrix products, absorb(): jnp.einsum('grd,sgd->grs', grouped, keys, preferred_element_type=jnp.floa...  5.75 us
    reduce_sum x8, other arithmetic, absorb(): total = total * shrink + jnp.sum(weights, axis=-1, keepdims=True)  5.68 us
  transfers between devices with their start and end apart: 1, of which 1 were waited for; matrix products, arithmetic and copies ran while one was open for 2% of the time, Pallas kernels for 0%

profile of v1, /device:TPU:56, one launch (start us, length us, event | category | flops | bytes accessed | tf_op | source)
XLA Modules:
  0.0 154.0 jit_solution(1761800651339547895)
XLA Ops:
  1.4 14.3 %all_to_all.20 = bf16[8,2,8,128]{3,0,1,2:T(8,128)(2,1)S(1)} all-to-all(bf16[8,2,8,128]{3,0,1,2:T(8,128)(2,1)S(1)} %copy.18), channel_id=1, replica_groups=mesh['resp'=64,'mp'=8] {'mp'}, dimensions={2} | all-to-all | bytes 65536 | tf_op jit(solution)/shard_map/all_to_all | solution.py:65
  15.7 1.8 %stack.5 = bf16[64,64,2,1,128]{4,1,2,3,0:T(8,128)(2,1)} broadcast(bf16[64,2,128]{2,0,1:T(8,128)(2,1)S(1)} %bitcast.105), dimensions={1,2,4} | broadcast | bytes 2129920 | tf_op jit(solution)/shard_map/stack | solution.py:67
  17.5 14.7 %all-to-all-start.1 = ((bf16[64,64,2,1,128]{4,1,2,3,0:T(8,128)(2,1)}), bf16[64,64,2,1,128]{4,1,2,3,0:T(8,128)(2,1)}, u32[]{:S(2)}, u32[]{:S(2)}) async-start(bf16[64,64,2,1,128]{4,1,2,3,0:T(8,128)(2,1)} %stack.5), calls=%async_computation.1 | async-start | bytes 4194304 | tf_op jit(solution)/shard_map/all_to_all | solution.py:67
  35.6 49.9 %all-to-all-done.1 = bf16[64,64,2,1,128]{4,1,2,3,0:T(8,128)(2,1)} async-done(((bf16[64,64,2,1,128]{4,1,2,3,0:T(8,128)(2,1)}), bf16[64,64,2,1,128]{4,1,2,3,0:T(8,128)(2,1)}, u32[]{:S(2)}, u32[]{:S(2)}) %all-to-all-start.1) | async-done | bytes 2097184 | tf_op jit(solution)/shard_map/all_to_all | solution.py:67
  85.5 3.1 %copy.20 = bf16[64,64,2,1,128]{4,1,0,2,3:T(8,128)(2,1)} copy(bf16[64,64,2,1,128]{4,1,2,3,0:T(8,128)(2,1)} %all-to-all-done.1) | data formatting | bytes 4194304 | tf_op jit(solution)/shard_map/all_to_all | solution.py:67
  88.6 29.5 %while.14 = (s32[]{:T(128)}, f32[1,2048,1]{1,2,0:T(1,128)S(1)}, f32[1,2048,1]{1,2,0:T(1,128)S(1)}, f32[1,2048,128]{2,1,0:T(8,128)S(1)}, bf16[8,512,2,1,128]{4,1,...) while((s32[]{:T(128)}, f32[1,2048,1]{1,2,0:T(1,128)S(1)}, f32[1,2048,1]{1,2,0:T(1,128)S(1)}, ...), condition=%wide.region_5.6_spmd, body=%wide.region_2.5_spmd.sunk | while | flops 545787904 | bytes 16121945 | solution.py:31
  88.6 1.0 dynamic-slice_bitcast_fusion.2
  91.1 1.2 fusion.32
  92.3 1.0 dynamic-slice_bitcast_fusion.2
  94.8 1.2 fusion.32
  96.0 1.0 dynamic-slice_bitcast_fusion.2
  98.4 1.2 fusion.32
  99.7 1.0 dynamic-slice_bitcast_fusion.2
  102.1 1.2 fusion.32
  103.3 1.0 dynamic-slice_bitcast_fusion.2
  105.8 1.2 fusion.32
  107.0 1.0 dynamic-slice_bitcast_fusion.2
  109.5 1.2 fusion.32
  110.7 1.0 dynamic-slice_bitcast_fusion.2
  113.2 1.2 fusion.32
  114.4 1.0 dynamic-slice_bitcast_fusion.2
  116.9 1.2 fusion.32
  118.4 1.0 multiply_reduce_fusion.1
  119.8 31.5 %psum.7 = f32[]{:T(128)} all-reduce(f32[]{:T(128)} %multiply_reduce_fusion.1), channel_id=1, replica_groups=mesh['resp'=64,'mp'=8] {'mp'}, use_global_device_ids=true, to_apply=%region_7.8 | all-reduce | flops 1 | bytes 8 | tf_op jit(solution)/shard_map/psum | solution.py:75
  (58 shorter events, 16.9 us)
Async XLA Ops:
  17.5 15.3 %copy-start = (bf16[256,8,128]{2,1,0:T(8,128)(2,1)S(1)}, bf16[256,8,128]{2,1,0:T(8,128)(2,1)}, u32[]{:S(2)}) copy-start(bf16[256,8,128]{2,1,0:T(8,128)(2,1)} %param.7) | copy-start | bytes 1572868
  17.5 15.4 %copy-start.1 = (bf16[256,2,1,128]{3,1,2,0:T(2,128)(2,1)S(1)}, bf16[256,2,1,128]{3,1,2,0:T(2,128)(2,1)}, u32[]{:S(2)}) copy-start(bf16[256,2,1,128]{3,1,2,0:T(2,128)(2,1)} %param.8) | copy-start | bytes 393220
  17.5 68.0 %all-to-all-start.1 = ((bf16[64,64,2,1,128]{4,1,2,3,0:T(8,128)(2,1)}), bf16[64,64,2,1,128]{4,1,2,3,0:T(8,128)(2,1)}, u32[]{:S(2)}, u32[]{:S(2)}) async-start(bf16[64,64,2,1,128]{4,1,2,3,0:T(8,128)(2,1)} %stack.5), calls=%async_computation.1 | async-start | bytes 4194304 | tf_op jit(solution)/shard_map/all_to_all | solution.py:67
  88.6 29.8 %copy-start.2 = (f32[1024]{0:T(1024)S(1)}, f32[1024]{0:T(1024)}, u32[]{:S(2)}) copy-start(f32[1024]{0:T(1024)} %param.11) | copy-start | bytes 12292
